TPU v7x, 256 devices: a whole 4x4x8 slice. The times are simulated.
256 devices in a mesh: shards: 32 (over y, z), tensor: 2 (over core), sections: 4 (over x).
Axes of the slice: x: 4, y: 4, z: 8, core: 2. Of those that a mesh axis runs over, the one named last changes fastest.
Arguments:
- in_inputs: bfloat16 [4, 32, 1, 512, 768], P('sections', 'shards'), may hold values from -6 to 6
- in_cotangents: bfloat16 [4, 32, 1, 512, 1792], P('sections', 'shards', None, None, 'tensor'), may hold values from -1536 to 1536
- out_inputs: bfloat16 [4, 32, 1, 512, 1536], P('sections', 'shards', None, None, 'tensor'), may hold values from -6 to 6
- out_cotangents: bfloat16 [4, 32, 1, 512, 768], P('sections', 'shards'), may hold values from -1536 to 1536
- token_counts: int32 [32, 1], P('shards'), may hold values from 1 to 512, as said below
- in_error: float32 [4, 32, 768, 1792], P('sections', 'shards', None, 'tensor'), may hold values from -3 to 3
- out_error: float32 [4, 32, 1536, 768], P('sections', 'shards', 'tensor'), may hold values from -3 to 3
- in_query: float32 [4, 1792, 32], P('sections', 'tensor'), may hold values from -6 to 6
- out_query: float32 [4, 768, 32], P('sections'), may hold values from -6 to 6
- vec_grads: float32 [4, 32, 10568], P('sections', 'shards', 'tensor'), may hold values from -384 to 384
- in_weight: float32 [4, 768, 1792], P('sections', 'shards', 'tensor'), may hold values from -3 to 3
- in_moment: float32 [4, 768, 1792], P('sections', 'shards', 'tensor'), may hold values from -3 to 3
- out_weight: float32 [4, 1536, 768], P('sections', 'tensor', 'shards'), may hold values from -3 to 3
- out_moment: float32 [4, 1536, 768], P('sections', 'tensor', 'shards'), may hold values from -3 to 3
- vec_weight: float32 [4, 10568], P('sections', 'tensor'), may hold values from -3 to 3
- vec_moment: float32 [4, 10568], P('sections', 'tensor'), may hold values from -3 to 3
Outputs:
- new_in_error: float32 [4, 32, 768, 1792], P('sections', 'shards', None, 'tensor')
- new_out_error: float32 [4, 32, 1536, 768], P('sections', 'shards', 'tensor')
- new_in_weight: float32 [4, 768, 1792], P('sections', 'shards', 'tensor')
- new_in_moment: float32 [4, 768, 1792], P('sections', 'shards', 'tensor')
- new_out_weight: float32 [4, 1536, 768], P('sections', 'tensor', 'shards')
- new_out_moment: float32 [4, 1536, 768], P('sections', 'tensor', 'shards')
- new_vec_weight: float32 [4, 10568], P('sections', 'tensor')
- new_vec_moment: float32 [4, 10568], P('sections', 'tensor')
Inputs may be any that keep to these rules, and one draw needn't show every extreme that they name: `token_counts`: each count is between 1 and 512; some micro-batch is full.
All inputs are finite; a program needn't handle non-finite values.
Results may differ from a plain program's by a relative error of at most 0.0003.
Values sent between devices are 32-bit elements; how exact they have to be, the bound alone decides.
No kernel may reach another device: no remote copies, remote signals or barrier semaphores. Data moves between devices by JAX's collectives and lax.ppermute only.
A program may use at most 64 MiB of HBM per device.

v0:
```python
import jax
import jax.numpy as jnp
from jax import lax
from jax.sharding import PartitionSpec as P


def triangular_apply(left, gram):
    factor = jnp.linalg.cholesky(gram)
    return jax.scipy.linalg.solve_triangular(factor, left.T, lower=True).T


def gradient(inputs, cotangents, valid):
    width_a = inputs.shape[-1]
    width_b = cotangents.shape[-1]
    masked = cotangents[0, 0] * valid[..., None]
    return lax.dot_general(
        inputs[0, 0].reshape(-1, width_a),
        masked.reshape(-1, width_b),
        (((0,), (0,)), ((), ())),
        preferred_element_type=jnp.float32,
    )


def local(
    in_inputs,
    in_cotangents,
    out_inputs,
    out_cotangents,
    token_counts,
    in_error,
    out_error,
    in_query,
    out_query,
    vec_grads,
    in_weight,
    in_moment,
    out_weight,
    out_moment,
    vec_weight,
    vec_moment,
):
    highest = lax.Precision.HIGHEST
    contract = (((0,), (0,)), ((), ()))
    replicas = lax.axis_size("shards")
    shard_index = lax.axis_index("shards")
    position = jnp.arange(in_inputs.shape[3], dtype=jnp.int32)
    valid = (position[None, :] < token_counts[0][:, None]).astype(jnp.bfloat16)
    total = lax.psum(jnp.sum(token_counts).astype(jnp.float32), "shards")
    work_in = gradient(in_inputs, in_cotangents, valid) / total + in_error[0, 0]
    work_out = gradient(out_inputs, out_cotangents, valid) / total + out_error[0, 0]
    part_in = jnp.dot(work_in, in_query[0], precision=highest)
    part_out = jnp.dot(work_out, out_query[0], precision=highest)
    vec_part = vec_grads[0, 0]
    left_in = lax.psum(part_in, ("shards", "tensor"))
    left_out, vec_total = lax.psum((part_out, vec_part), "shards")
    ortho_in = triangular_apply(left_in, jnp.dot(left_in.T, left_in, precision=highest))
    gram_part = jnp.dot(left_out.T, left_out, precision=highest)
    ortho_out = triangular_apply(left_out, lax.psum(gram_part, "tensor"))
    right_part_in = lax.dot_general(work_in, ortho_in, contract, precision=highest)
    right_part_out = lax.dot_general(work_out, ortho_out, contract, precision=highest)
    right_in = lax.psum(right_part_in, "shards")
    right_out = lax.psum(right_part_out, ("shards", "tensor"))
    right_in = right_in / replicas
    right_out = right_out / replicas
    approx_in = jnp.dot(ortho_in, right_in.T, precision=highest)
    approx_out = jnp.dot(ortho_out, right_out.T, precision=highest)
    new_in_error = (work_in - approx_in)[None, None]
    new_out_error = (work_out - approx_out)[None, None]
    vec_mean = vec_total / total
    local_square = (
        jnp.sum(right_in * right_in)
        + 0.5 * jnp.sum(right_out * right_out)
        + jnp.sum(vec_mean * vec_mean)
    )
    square_sum = lax.psum(local_square, ("tensor", "sections"))
    factor = 1024.0 / jnp.sqrt(square_sum + 1e-06)
    row_count = in_weight.shape[1]
    shard_in = lax.dynamic_slice_in_dim(approx_in, shard_index * row_count, row_count, 0)
    col_count = out_weight.shape[2]
    shard_out = lax.dynamic_slice_in_dim(approx_out, shard_index * col_count, col_count, 1)
    new_in_moment = 0.9 * in_moment + factor * shard_in[None]
    new_out_moment = 0.9 * out_moment + factor * shard_out[None]
    new_vec_moment = 0.9 * vec_moment + factor * vec_mean[None]
    return (
        new_in_error,
        new_out_error,
        in_weight - 0.1 * new_in_moment,
        new_in_moment,
        out_weight - 0.1 * new_out_moment,
        new_out_moment,
        vec_weight - 0.1 * new_vec_moment,
        new_vec_moment,
    )


def solution(mesh):
    return jax.shard_map(
        local,
        mesh=mesh,
        in_specs=(
            P("sections", "shards", None, None, None),
            P("sections", "shards", None, None, "tensor"),
            P("sections", "shards", None, None, "tensor"),
            P("sections", "shards", None, None, None),
            P("shards", None),
            P("sections", "shards", None, "tensor"),
            P("sections", "shards", "tensor", None),
            P("sections", "tensor", None),
            P("sections", None, None),
            P("sections", "shards", "tensor"),
            P("sections", "shards", "tensor"),
            P("sections", "shards", "tensor"),
            P("sections", "tensor", "shards"),
            P("sections", "tensor", "shards"),
            P("sections", "tensor"),
            P("sections", "tensor"),
        ),
        out_specs=(
            P("sections", "shards", None, "tensor"),
            P("sections", "shards", "tensor", None),
            P("sections", "shards", "tensor"),
            P("sections", "shards", "tensor"),
            P("sections", "tensor", "shards"),
            P("sections", "tensor", "shards"),
            P("sections", "tensor"),
            P("sections", "tensor"),
        ),
        check_vma=False,
    )
```

profile of v0, /device:TPU:1, one launch (start us, length us, event | category | flops | bytes accessed | tf_op | source)
XLA Modules:
  0.0 715.9 jit_solution(11773875914962923723)
XLA Ops:
  8.7 3.0 copy.27
  11.8 118.9 %all-reduce.1 = (f32[]{:T(128)}, f32[5284]{0:T(1024)}) all-reduce(f32[]{:T(128)S(6)} %convert_element_type.13, f32[5284]{0:T(1024)S(1)} %reduce.4), channel_id=1, replica_groups=mesh['shards'=32,'tensor'=2,'sections'=4] {'shards'}, use_global_device_ids=true, to_apply=%region_0.0 | all-reduce | flops 5285 | bytes 42280 | tf_op jit(solution)/shard_map/psum | solution.py:48
  130.7 3.7 bitcast_add_fusion.1
  136.7 3.3 copy.24
  140.0 3.8 bitcast_add_fusion
  143.8 2.2 fusion.8
  146.0 151.1 %all-reduce.8.cloned.1.call-done = f32[768,32]{0,1:T(8,128)} async-done(((f32[768,32]{0,1:T(8,128)}), f32[768,32]{0,1:T(8,128)}) %all-reduce.8.cloned.1.call-update) | async-done | bytes 98320 | tf_op jit(solution)/shard_map/psum | solution.py:55
  299.0 8.8 %psum.60 = f32[32,32]{0,1:T(8,128)S(1)} all-reduce(f32[32,32]{0,1:T(8,128)} %fusion.33), channel_id=1, replica_groups=mesh['shards'=32,'tensor'=2,'sections'=4] {'tensor'}, use_global_device_ids=true, to_apply=%region_6.0 | all-reduce | flops 1024 | bytes 8192 | tf_op jit(solution)/shard_map/psum | solution.py:58
  309.8 3.6 cholesky.55
  315.4 3.2 custom-call.7
  320.4 4.5 fusion.34
  327.1 174.8 %all-reduce.10.cloned.1.call-done = (f32[768,32]{0,1:T(8,128)}, f32[768,32]{0,1:T(8,128)}) async-done(((f32[768,32]{0,1:T(8,128)}, f32[768,32]{0,1:T(8,128)}), (f32[768,32]{0,1:T(8,128)}, f32[768,32]{0,1:T(8,128)})) %all-reduce.10.cloned.1.call-update) | async-done | bytes 196624 | tf_op jit(solution)/shard_map/psum | solution.py:54
  501.9 4.4 fusion.18
  509.5 3.6 cholesky.44
  515.1 3.2 custom-call.6
  520.1 3.1 fusion.32
  523.2 4.1 subtract_bitcast_fusion.1
  528.6 132.9 %all-reduce.6.cloned.1.call-done = f32[896,32]{0,1:T(8,128)} async-done(((f32[896,32]{0,1:T(8,128)}), f32[896,32]{0,1:T(8,128)}) %all-reduce.6.cloned.1.call-update) | async-done | bytes 114704 | tf_op jit(solution)/shard_map/psum | solution.py:61
  664.3 3.0 copy.31
  667.4 20.2 %psum.63 = f32[]{:T(128)} all-reduce(f32[]{:T(128)S(6)} %add.56), channel_id=1, replica_groups=mesh['shards'=32,'tensor'=2,'sections'=4] {'tensor','sections'}, use_global_device_ids=true, to_apply=%region_12.15 | all-reduce | flops 1 | bytes 8 | tf_op jit(solution)/shard_map/psum | solution.py:75
  690.2 4.9 fusion.10
  695.1 3.3 copy.26
  698.4 3.7 subtract_bitcast_fusion
  702.1 3.4 copy.30
  (58 shorter events, 27.8 us)
Async XLA Ops:
  7.2 132.9 %copy-start = (bf16[1,1,1,512,768]{4,3,2,1,0:T(8,128)(2,1)S(1)}, bf16[1,1,1,512,768]{4,3,2,1,0:T(8,128)(2,1)}, u32[]{:S(2)}) copy-start(bf16[1,1,1,512,768]{4,3,2,1,0:T(8,128)(2,1)} %param.19) | copy-start | bytes 2359300
  7.2 290.0 %all-reduce.8.cloned.1.call-start = ((), (), s32[]{:S(2)}) async-start(), calls=%async_computation.1 | async-start | bytes 196608 | tf_op jit(solution)/shard_map/psum | solution.py:55
  130.7 3.7 copy-start.6
  134.5 2.3 copy-start.1
  136.7 365.2 %all-reduce.10.cloned.1.call-start = ((), (), s32[]{:S(2)}) async-start(), calls=%async_computation.2 | async-start | bytes 393216 | tf_op jit(solution)/shard_map/psum | solution.py:54
  140.0 3.8 copy-start.5
  319.7 0.6 copy-start.3
  324.9 336.6 %all-reduce.6.cloned.1.call-start = ((), (), s32[]{:S(2)}) async-start(), calls=%async_computation | async-start | bytes 229376 | tf_op jit(solution)/shard_map/psum | solution.py:61
  519.4 0.6 copy-start.2
  523.2 4.1 copy-start.4
  702.1 3.4 copy-start.10
  702.1 3.4 copy-start.11
  702.1 5.0 copy-start.8
  702.1 5.0 copy-start.9
  702.1 6.6 copy-start.7
  702.1 6.6 copy-start.12
  702.1 6.6 copy-start.13
Sparse Core Ops, SparseCore 0:
  136.8 160.3 all-reduce.7
  325.0 176.8 all-reduce.9
  523.3 138.1 all-reduce.5
where the time goes:
time: 717 us; the launch traced here: 716 us
  waiting for transfers between devices  459 us (64%)
  blocking collectives  148 us (21%)
  other arithmetic  38.6 us (5%)
  matrix products  34.2 us (5%)
  local copies, waits for them, and re-layouts  18.8 us (3%)
  between operations  17.3 us (2%)
    psum x1, waiting for transfers between devices, local(): left_in = lax.psum(part_in, ('shards', 'tensor'))  175 us
    psum x1, waiting for transfers between devices, local(): left_out, vec_total = lax.psum((part_out, vec_part), 'shards')  151 us
    psum x1, waiting for transfers between devices, local(): right_in = lax.psum(right_part_in, 'shards')  133 us
    psum x1, blocking collectives, local(): total = lax.psum(jnp.sum(token_counts).astype(jnp.float32), 'shards')  119 us
    psum x1, blocking collectives, local(): square_sum = lax.psum(local_square, ('tensor', 'sections'))  20.2 us
  transfers between devices with their start and end apart: 3, of which 3 were waited for; matrix products, arithmetic and copies ran while one was open for 2% of the time, Pallas kernels for 0%

commit v1 on v0

--- a/solution.py
+++ b/solution.py
@@ -58,7 +58,11 @@
     ortho_out = triangular_apply(left_out, lax.psum(gram_part, "tensor"))
     right_part_in = lax.dot_general(work_in, ortho_in, contract, precision=highest)
     right_part_out = lax.dot_general(work_out, ortho_out, contract, precision=highest)
-    right_in = lax.psum(right_part_in, "shards")
+    right_in = right_part_in
+    for hop in (1, 2, 4, 8, 16):
+        right_in = right_in + lax.ppermute(
+            right_in, "shards", [(dev, dev ^ hop) for dev in range(32)]
+        )
     right_out = lax.psum(right_part_out, ("shards", "tensor"))
     right_in = right_in / replicas
     right_out = right_out / replicas

time: 717 us -> 608 us (0.85)
  waiting for transfers between devices: 459 us -> 338 us
  starting transfers between devices: 0.3 us -> 12.1 us
    psum x1 -> x0, waiting for transfers between devices: 133 us -> none  [local(): right_in = lax.psum(right_part_in, 'shards')]
    ppermute x0 -> x5, starting transfers between devices: none -> 12 us  [local(): lax.ppermute(right_in, 'shards', [(dev, dev ^ hop) for dev in range(32)])]
    ppermute x0 -> x5, waiting for transfers between devices: none -> 9.38 us  [local(): lax.ppermute(right_in, 'shards', [(dev, dev ^ hop) for dev in range(32)])]
  transfers between devices with their start and end apart: 3 -> 7, of which waited for: 3 -> 6; matrix products, arithmetic and copies ran while one was open for 2% -> 3% of each run, Pallas kernels for 0% -> 0%
where the time goes in v1:
time: 608 us; the launch traced here: 607 us
  waiting for transfers between devices  338 us (56%)
  blocking collectives  149 us (25%)
  other arithmetic  38.2 us (6%)
  matrix products  32.9 us (5%)
  local copies, waits for them, and re-layouts  18.8 us (3%)
  between operations  17.6 us (3%)
  starting transfers between devices  12.1 us (2%)
    psum x1, waiting for transfers between devices, local(): left_in = lax.psum(part_in, ('shards', 'tensor'))  177 us
    psum x1, waiting for transfers between devices, local(): left_out, vec_total = lax.psum((part_out, vec_part), 'shards')  151 us
    psum x1, blocking collectives, local(): total = lax.psum(jnp.sum(token_counts).astype(jnp.float32), 'shards')  119 us
    psum x1, blocking collectives, local(): square_sum = lax.psum(local_square, ('tensor', 'sections'))  21.7 us
    unnamed x36, local copies, waits for them, and re-layouts  14.1 us
  transfers between devices with their start and end apart: 7, of which 6 were waited for; matrix products, arithmetic and copies ran while one was open for 3% of the time, Pallas kernels for 0%

profile of v1, /device:TPU:1, one launch (start us, length us, event | category | flops | bytes accessed | tf_op | source)
XLA Modules:
  0.0 607.1 jit_solution(5716441034992508917)
XLA Ops:
  8.7 3.0 copy.27
  11.8 118.9 %all-reduce.1 = (f32[]{:T(128)}, f32[5284]{0:T(1024)}) all-reduce(f32[]{:T(128)S(6)} %convert_element_type.13, f32[5284]{0:T(1024)S(1)} %reduce.4), channel_id=1, replica_groups=mesh['shards'=32,'tensor'=2,'sections'=4] {'shards'}, use_global_device_ids=true, to_apply=%region_0.0 | all-reduce | flops 5285 | bytes 42280 | tf_op jit(solution)/shard_map/psum | solution.py:48
  130.7 3.7 bitcast_add_fusion.1
  136.7 3.3 copy.24
  140.0 3.8 bitcast_add_fusion
  146.0 151.1 %all-reduce.5.cloned.1.call-done = f32[768,32]{0,1:T(8,128)} async-done(((f32[768,32]{0,1:T(8,128)}), f32[768,32]{0,1:T(8,128)}) %all-reduce.5.cloned.1.call-update) | async-done | bytes 98320 | tf_op jit(solution)/shard_map/psum | solution.py:55
  299.0 8.8 %psum.52 = f32[32,32]{0,1:T(8,128)S(1)} all-reduce(f32[32,32]{0,1:T(8,128)} %fusion.31), channel_id=1, replica_groups=mesh['shards'=32,'tensor'=2,'sections'=4] {'tensor'}, use_global_device_ids=true, to_apply=%region_5.0 | all-reduce | flops 1024 | bytes 8192 | tf_op jit(solution)/shard_map/psum | solution.py:58
  309.8 3.6 cholesky.55
  315.4 3.2 custom-call.7
  320.4 4.5 fusion.32
  324.9 177.5 %all-reduce.7.cloned.1.call-done = (f32[768,32]{0,1:T(8,128)}, f32[768,32]{0,1:T(8,128)}) async-done(((f32[768,32]{0,1:T(8,128)}, f32[768,32]{0,1:T(8,128)}), (f32[768,32]{0,1:T(8,128)}, f32[768,32]{0,1:T(8,128)})) %all-reduce.7.cloned.1.call-update) | async-done | bytes 196624 | tf_op jit(solution)/shard_map/psum | solution.py:54
  505.6 3.6 cholesky.44
  511.2 3.2 custom-call.6
  516.2 3.2 fusion.30
  524.2 4.6 collective-permute-start.1
  531.0 5.8 collective-permute-start.2
  536.9 3.0 fusion.16
  546.1 4.7 collective-permute-done.4
  553.7 3.0 copy.31
  556.7 21.7 %psum.55 = f32[]{:T(128)} all-reduce(f32[]{:T(128)S(6)} %add.74), channel_id=1, replica_groups=mesh['shards'=32,'tensor'=2,'sections'=4] {'tensor','sections'}, use_global_device_ids=true, to_apply=%region_11.14 | all-reduce | flops 1 | bytes 8 | tf_op jit(solution)/shard_map/psum | solution.py:79
  581.1 4.9 fusion.19
  586.0 3.3 copy.26
  589.3 3.7 subtract_bitcast_fusion
  593.0 3.4 copy.30
  (73 shorter events, 39.9 us)
Async XLA Ops:
  7.2 132.9 %copy-start = (bf16[1,1,1,512,768]{4,3,2,1,0:T(8,128)(2,1)S(1)}, bf16[1,1,1,512,768]{4,3,2,1,0:T(8,128)(2,1)}, u32[]{:S(2)}) copy-start(bf16[1,1,1,512,768]{4,3,2,1,0:T(8,128)(2,1)} %param.19) | copy-start | bytes 2359300
  7.2 290.0 %all-reduce.5.cloned.1.call-start = ((), (), s32[]{:S(2)}) async-start(), calls=%async_computation | async-start | bytes 196608 | tf_op jit(solution)/shard_map/psum | solution.py:55
  130.7 3.7 copy-start.8
  134.5 2.3 copy-start.1
  136.7 365.7 %all-reduce.7.cloned.1.call-start = ((), (), s32[]{:S(2)}) async-start(), calls=%async_computation.1 | async-start | bytes 393216 | tf_op jit(solution)/shard_map/psum | solution.py:54
  140.0 3.8 copy-start.7
  319.7 0.6 copy-start.5
  515.5 0.6 copy-start.4
  519.3 4.0 collective-permute-start
  520.7 19.4 %copy-start.2 = (f32[768,768]{0,1:T(8,128)S(1)}, f32[768,768]{0,1:T(8,128)}, u32[]{:S(2)}) copy-start(f32[768,768]{0,1:T(8,128)} %copy-done.1) | copy-start | bytes 7077892
  524.2 6.8 %collective-permute-start.1 = (f32[896,32]{0,1:T(8,128)S(1)}, f32[896,32]{0,1:T(8,128)S(1)}, u32[]{:S(2)}, u32[]{:S(2)}) collective-permute-start(f32[896,32]{0,1:T(8,128)S(1)} %add.67), channel_id=1, source_target_pairs={{0,16},{8,24},{16,0},{24,8},{32,48},{40,56},{48,32},{56,40},{64,80... | collective-permute-start | bytes 344072 | tf_op jit(solution)/shard_map/ppermute | solution.py:63
  531.0 8.9 %collective-permute-start.2 = (f32[896,32]{0,1:T(8,128)S(1)}, f32[896,32]{0,1:T(8,128)S(1)}, u32[]{:S(2)}, u32[]{:S(2)}) collective-permute-start(f32[896,32]{0,1:T(8,128)S(1)} %add.68), channel_id=1, source_target_pairs={{0,32},{8,40},{16,48},{24,56},{32,0},{40,8},{48,16},{56,24},{64,96... | collective-permute-start | bytes 344072 | tf_op jit(solution)/shard_map/ppermute | solution.py:63
  539.9 2.2 copy-start.3
  539.9 4.8 copy-start.6
  540.0 4.0 collective-permute-start.3
  544.7 6.1 %collective-permute-start.4 = (f32[896,32]{0,1:T(8,128)}, f32[896,32]{0,1:T(8,128)}, u32[]{:S(2)}, u32[]{:S(2)}) collective-permute-start(f32[896,32]{0,1:T(8,128)} %add.70), channel_id=1, source_target_pairs={{0,128},{8,136},{16,144},{24,152},{32,160},{40,168},{48,176},{56,1... | collective-permute-start | bytes 344072 | tf_op jit(solution)/shard_map/ppermute | solution.py:63
  593.0 3.4 copy-start.12
  593.0 3.4 copy-start.13
  593.0 5.0 copy-start.10
  593.0 5.0 copy-start.11
  593.0 6.6 %copy-start.9 = (f32[5284]{0:T(1024)S(1)}, f32[5284]{0:T(1024)}, u32[]{:S(2)}) copy-start(f32[5284]{0:T(1024)} %broadcast_multiply_fusion) | copy-start | bytes 63412
  593.0 6.6 %copy-start.14 = (f32[1,5284]{1,0:T(1,128)S(1)}, f32[1,5284]{1,0:T(1,128)}, u32[]{:S(2)}) copy-start(f32[1,5284]{1,0:T(1,128)} %param.33) | copy-start | bytes 63412
  593.0 6.6 %copy-start.15 = (f32[1,5284]{1,0:T(1,128)S(1)}, f32[1,5284]{1,0:T(1,128)}, u32[]{:S(2)}) copy-start(f32[1,5284]{1,0:T(1,128)} %param.34) | copy-start | bytes 63412
Sparse Core Ops, SparseCore 0:
  136.8 160.3 all-reduce.4
  325.0 177.2 all-reduce.6
